TPU v7x, 512 devices: a whole 4x4x16 slice. The times are simulated.
512 devices in a mesh: seq: 64 (over x, z), tp: 8 (over y, core).
Axes of the slice: x: 4, y: 4, z: 16, core: 2. Of those that a mesh axis runs over, the one named last changes fastest.
Arguments:
- hidden_in: bfloat16 [8192, 2048], P('seq', 'tp'), may hold values from -3 to 3
- norm_gain: float32 [2048], replicated, may hold values from 0.1 to 1.9
- w_query: bfloat16 [2048, 2048], P(None, 'tp'), may hold values from -0.125 to 0.125
- w_key: bfloat16 [2048, 1024], P(None, 'tp'), may hold values from -0.125 to 0.125
- w_value: bfloat16 [2048, 1024], P(None, 'tp'), may hold values from -0.125 to 0.125
- w_headgate: bfloat16 [2048, 16], P(None, 'tp'), may hold values from -0.125 to 0.125
- w_out: bfloat16 [2048, 2048], P('tp'), may hold values from -0.125 to 0.125
- q_gain: float32 [128], replicated, may hold values from 1.5 to 4
- k_gain: float32 [128], replicated, may hold values from 0.1 to 1.9
- cache_keys: bfloat16 [2, 8192, 1024], P(None, 'seq', 'tp'), as said below
- cache_values: bfloat16 [2, 8192, 1024], P(None, 'seq', 'tp'), may hold values from -6 to 6
- cached_len: int32 [8], replicated, may hold values from 0 to 8192, as said below
- group_of: int32 [8], replicated, may hold values from 0 to 1, as said below
Outputs:
- layer_out: bfloat16 [8192, 2048], P('seq', 'tp')
Inputs may be any that keep to these rules, and one draw needn't show every extreme that they name: `cache_keys`: keys of the cached positions, of order one and larger. `cached_len`: some request attends to all 8192 cached positions of its prompt, and some to none. `group_of`: every shared prompt is used by some request.
All inputs are finite; a program needn't handle non-finite values.
Results may differ from a plain program's by a relative error of at most 0.018.
Values may be sent and summed in bfloat16 or wider, within the bound.
No kernel may reach another device: no remote copies, remote signals or barrier semaphores. Data moves between devices by JAX's collectives and lax.ppermute only.
A program may use at most 64 MiB of HBM per device.

v0:
```python
import math
import jax
import jax.numpy as jnp
from jax import lax
from jax.sharding import PartitionSpec as P

SPAN = 1024
norm_eps = 1e-06
rope_base = 1000000.0
masked_score = -1e30


def shifted(value, axis, by):
    peers = lax.axis_size(axis)
    pairs = [(i, i + by) for i in range(peers) if 0 <= i + by < peers]
    return lax.ppermute(value, axis, pairs)


def head_norm(vec, gain):
    return vec * lax.rsqrt(jnp.mean(vec * vec, -1, keepdims=True) + norm_eps) * gain


def rotate(vec, positions):
    half = vec.shape[-1] // 2
    freq = jnp.exp(
        jnp.arange(half, dtype=jnp.float32) * (-2.0 * math.log(rope_base) / vec.shape[-1])
    )
    angle = positions.astype(jnp.float32)[:, None] * freq[None, :]
    shape_out = (vec.shape[0],) + (1,) * (vec.ndim - 2) + (half,)
    cosine = jnp.cos(angle).reshape(shape_out)
    sine = jnp.sin(angle).reshape(shape_out)
    first = vec[..., :half]
    second = vec[..., half:]
    return jnp.concatenate([first * cosine - second * sine, second * cosine + first * sine], -1)


def attend(state_now, queries, keys_block, values_block, visible):
    running_max, running_sum, running_acc = state_now
    scores = jnp.einsum(
        "tcgd,kcd->tcgk", queries, keys_block, preferred_element_type=jnp.float32
    ) * queries.shape[-1] ** (-0.5)
    scores = jnp.where(visible[:, None, None, :], scores, masked_score)
    new_max = jnp.maximum(running_max, jnp.max(scores, -1))
    rescale = jnp.exp(running_max - new_max)
    expo = jnp.exp(scores - new_max[..., None])
    new_sum = running_sum * rescale + jnp.sum(expo, -1)
    update = jnp.einsum(
        "tcgk,kcd->tcgd",
        expo.astype(jnp.bfloat16),
        values_block,
        preferred_element_type=jnp.float32,
    )
    return (new_max, new_sum, running_acc * rescale[..., None] + update)


def per_device(
    hidden_in,
    norm_gain,
    w_query,
    w_key,
    w_value,
    w_headgate,
    w_out,
    q_gain,
    k_gain,
    cache_keys,
    cache_values,
    cached_len,
    group_of,
):
    tok_rows = hidden_in.shape[0]
    head_dim = q_gain.shape[0]
    kv_local = w_key.shape[1] // head_dim
    heads_local = w_query.shape[1] // head_dim
    group_size = heads_local // kv_local
    per_request = SPAN // tok_rows
    seq_size = lax.axis_size("seq")
    req_count = seq_size // per_request
    gathered = lax.all_gather(hidden_in, "tp", axis=1, tiled=True)
    widened = gathered.astype(jnp.float32)
    normed = (
        widened * lax.rsqrt(jnp.mean(widened * widened, -1, keepdims=True) + norm_eps) * norm_gain
    ).astype(jnp.bfloat16)
    seq_index = lax.axis_index("seq")
    local_part = seq_index // req_count
    request = seq_index % req_count
    length = cached_len[request]
    group_id = group_of[request]
    positions = length + local_part * tok_rows + jnp.arange(tok_rows, dtype=jnp.int32)
    query_raw = jnp.dot(normed, w_query, preferred_element_type=jnp.float32).reshape(
        tok_rows, kv_local, group_size, head_dim
    )
    queries = rotate(head_norm(query_raw, q_gain), positions).astype(jnp.bfloat16)
    key_raw = jnp.dot(normed, w_key, preferred_element_type=jnp.float32).reshape(
        tok_rows, kv_local, head_dim
    )
    keys_new = rotate(head_norm(key_raw, k_gain), positions).astype(jnp.bfloat16)
    values_new = (
        jnp.dot(normed, w_value, preferred_element_type=jnp.float32)
        .astype(jnp.bfloat16)
        .reshape(tok_rows, kv_local, head_dim)
    )
    gates = jax.nn.sigmoid(jnp.dot(normed, w_headgate, preferred_element_type=jnp.float32)).reshape(
        tok_rows, kv_local, group_size
    )
    state_now = (
        jnp.full((tok_rows, kv_local, group_size), masked_score, jnp.float32),
        jnp.zeros((tok_rows, kv_local, group_size), jnp.float32),
        jnp.zeros((tok_rows, kv_local, group_size, head_dim), jnp.float32),
    )
    row_ids = jnp.arange(tok_rows, dtype=jnp.int32)
    state_now = attend(
        state_now, queries, keys_new, values_new, row_ids[None, :] <= row_ids[:, None]
    )
    all_seen = jnp.ones((1, tok_rows), bool)
    for distance in range(1, per_request):
        earlier_keys, earlier_values = shifted((keys_new, values_new), "seq", distance * req_count)
        state_now = lax.cond(
            local_part >= distance,
            lambda state_in: attend(state_in, queries, earlier_keys, earlier_values, all_seen),
            lambda state_in: state_in,
            state_now,
        )
    keys_piece = lax.all_gather(cache_keys, "seq", axis=1, tiled=True)
    values_piece = lax.all_gather(cache_values, "seq", axis=1, tiled=True)
    row_count = keys_piece.shape[1]
    keys_block = lax.dynamic_index_in_dim(keys_piece, group_id, 0, keepdims=False).reshape(
        row_count, kv_local, head_dim
    )
    values_block = lax.dynamic_index_in_dim(values_piece, group_id, 0, keepdims=False).reshape(
        row_count, kv_local, head_dim
    )
    visible = (jnp.arange(row_count, dtype=jnp.int32) < length)[None, :]
    state_now = lax.cond(
        jnp.int32(0) < length,
        lambda state_old: attend(state_old, queries, keys_block, values_block, visible),
        lambda state_old: state_old,
        state_now,
    )
    running_max, running_sum, running_acc = state_now
    mixed = (
        (running_acc / running_sum[..., None] * gates[..., None])
        .astype(jnp.bfloat16)
        .reshape(tok_rows, heads_local * head_dim)
    )
    partial_out = jnp.dot(mixed, w_out, preferred_element_type=jnp.float32)
    summed = lax.psum_scatter(
        partial_out.astype(jnp.bfloat16), "tp", scatter_dimension=1, tiled=True
    ).astype(jnp.float32)
    return (hidden_in.astype(jnp.float32) + summed).astype(jnp.bfloat16)


def solution(mesh):
    in_specs = (
        P("seq", "tp"),
        P(),
        P(None, "tp"),
        P(None, "tp"),
        P(None, "tp"),
        P(None, "tp"),
        P("tp", None),
        P(),
        P(),
        P(None, "seq", "tp"),
        P(None, "seq", "tp"),
        P(),
        P(),
    )
    out_specs = P("seq", "tp")
    return jax.shard_map(
        per_device, mesh=mesh, in_specs=in_specs, out_specs=out_specs, check_vma=False
    )
```

profile of v0, /device:TPU:2, one launch (start us, length us, event | category | flops | bytes accessed | tf_op | source)
XLA Modules:
  0.0 363.7 jit_solution(5019279901672864416)
XLA Ops:
  6.6 0.7 all-gather.3.cloned.1.call-update
  7.3 1.6 copy.86
  9.0 13.8 %all_gather.9 = bf16[128,2048]{1,0:T(8,128)(2,1)S(1)} all-gather(bf16[128,256]{1,0:T(8,128)(2,1)} %param.29), channel_id=1, replica_groups=mesh['seq'=64,'tp'=8] {'tp'}, dimensions={1}, use_global_device_ids=true | all-gather | bytes 589824 | tf_op jit(solution)/shard_map/all_gather | solution.py:79
  22.8 0.2 fusion.112
  23.0 1.4 convolution_convert_fusion.1
  24.4 17.3 %collective-permute-start.9 = (bf16[128,1,128]{2,0,1:T(8,128)(2,1)S(1)}, bf16[128,1,128]{2,0,1:T(8,128)(2,1)S(1)}, u32[]{:S(2)}, u32[]{:S(2)}) collective-permute-start(bf16[128,1,128]{2,0,1:T(8,128)(2,1)S(1)} %bitcast.382), channel_id=1, source_target_pairs={{0,320},{8,328},{16,336},{24,344},{32,352},{40,360},{48,368},{56,3... | collective-permute-start | bytes 98312 | tf_op jit(solution)/shard_map/ppermute | solution.py:16
  41.7 1.3 collective-permute-start.7
  43.0 1.3 collective-permute-start.5
  44.3 2.5 collective-permute-start.3
  46.8 2.5 collective-permute-start.1
  49.4 1.6 fusion.139
  51.1 0.2 multiply_reduce_fusion
  51.3 1.3 dynamic_slice.27
  53.4 1.5 multiply_reduce_fusion.1
  54.9 0.7 multiply_bitcast_fusion
  55.6 0.2 fusion.129
  55.9 0.3 multiply_cosine_fusion
  56.2 0.8 fusion.115
  57.0 0.3 fusion.151
  57.4 0.2 fusion.107
  57.6 0.3 fusion.111
  57.9 1.3 collective-permute-start.6
  59.2 1.8 collective-permute-start.4
  61.0 1.9 collective-permute-start.2
  63.0 11.6 %collective-permute-start = (bf16[128,1,128]{0,2,1:T(8,128)(2,1)S(1)}, bf16[128,1,128]{0,2,1:T(8,128)(2,1)S(1)}, u32[]{:S(2)}, u32[]{:S(2)}) collective-permute-start(bf16[128,1,128]{0,2,1:T(8,128)(2,1)S(1)} %pad_maximum_fusion.1), channel_id=1, source_target_pairs={{0,64},{8,72},{16,80},{24,88},{32,96},{40,104},{48,112},{56,120},{... | collective-permute-start | bytes 98312 | tf_op jit(solution)/shard_map/ppermute | solution.py:16
  74.6 0.7 collective-permute-start.13
  75.3 0.7 collective-permute-start.11
  76.0 0.7 collective-permute-start.12
  76.7 0.7 collective-permute-start.10
  77.3 1.6 collective-permute-done
  78.9 1.3 collective-permute-start.8
  81.0 0.6 conditional.8
  81.1 0.2 fusion.144
  81.3 0.2 fusion.1
  81.7 0.5 conditional.9
  81.7 0.2 fusion.145
  81.9 0.2 fusion.12
  82.3 82.6 %all-gather.3.cloned.1.call-done = bf16[2,8192,128]{2,1,0:T(8,128)(2,1)} async-done(((bf16[2,128,128]{2,1,0:T(8,128)(2,1)}), bf16[2,8192,128]{2,1,0:T(8,128)(2,1)}) %all-gather.3.cloned.1.call-update) | async-done | bytes 4194320 | tf_op jit(solution)/shard_map/all_gather | solution.py:124
  164.9 143.5 %all-gather.5.cloned.1.call-done = bf16[2,8192,128]{1,2,0:T(8,128)(2,1)} async-done(((bf16[2,128,128]{1,2,0:T(8,128)(2,1)}), bf16[2,8192,128]{1,2,0:T(8,128)(2,1)}) %all-gather.5.cloned.1.call-update) | async-done | bytes 4194320 | tf_op jit(solution)/shard_map/all_gather | solution.py:125
  308.4 11.9 %conditional.15 = (f32[128,1,2]{0,2,1:T(2,128)S(1)}, f32[128,1,2,128]{0,3,2,1:T(8,128)S(1)}) conditional(s32[]{:T(128)} %convert_element_type.107, (f32[128,1,2]{0,2,1:T(2,128)S(1)}, f32[128,1,2,128]{3,0,2,1:T(8,128)S(1)}) %tuple.71, (s32[]{:T(128)}, s32[8192]{0:T(1024)S(1)}, s32[8]{0:T(128)S(1)}, s32[]{:T(128)}, bf16[2,8192,128]{2,1,0:T(8,128)(2,1)}, ...), branch_computations={%region_33.34_spmd, %region_34.37_spmd} | conditional | flops 1088496640 | bytes 46790756 | solution.py:134
  308.4 0.6 dynamic_slice.23
  311.0 0.7 broadcast_compare_fusion
  311.8 5.8 %fusion.143 = (f32[128,2]{0,1:T(2,128)S(1)}, f32[128,1,2,8192]{0,3,2,1:T(8,128)S(1)}) fusion(bf16[128,1,2,128]{3,0,2,1:T(8,128)(2,1)S(1)} %get-tuple-element.286, bf16[2,8192,128]{2,1,0:T(8,128)(2,1)} %get-tuple-element.283, s32[]{:T(128)S(6)} %select_n.37, pred[8192]{0:T(1024)(128)(4,1)S(1)} %broadcast_compare_fusion), kind=kOutput, calls=%fused_computation.202 | convolution fusion | flops 543162112 | bytes 10560516 | tf_op jit(solution)/shard_map/cond/branch_1_fun/tcgd,kcd->tcgk/dot_general | solution.py:39
  317.6 1.6 fusion.95
  319.2 1.1 fusion.81
  320.4 1.1 convolution_convert_fusion
  321.6 34.1 %reduce-scatter.2.cloned.1.call-done = bf16[128,256]{1,0:T(8,128)(2,1)} async-done(((bf16[128,2048]{1,0:T(8,128)(2,1)}), bf16[128,256]{1,0:T(8,128)(2,1)}) %reduce-scatter.2.cloned.1.call-update) | async-done | bytes 65552 | tf_op jit(solution)/shard_map/reduce_scatter | solution.py:147
  355.6 1.5 add_convert_fusion
  (63 shorter events, 1.1 us)
Async XLA Ops:
  6.5 313.9 %copy-start = (bf16[256,2048]{1,0:T(8,128)(2,1)S(1)}, bf16[256,2048]{1,0:T(8,128)(2,1)}, u32[]{:S(2)}) copy-start(bf16[256,2048]{1,0:T(8,128)(2,1)} %param.35) | copy-start | bytes 3145732
  6.5 51.0 %copy-start.3 = (f32[2048]{0:T(1024)S(1)}, f32[2048]{0:T(1024)}, u32[]{:S(2)}) copy-start(f32[2048]{0:T(1024)} %param.30) | copy-start | bytes 24580
  6.5 51.0 %copy-start.4 = (bf16[2048,2]{0,1:T(2,128)(2,1)S(1)}, bf16[2048,2]{0,1:T(2,128)(2,1)}, u32[]{:S(2)}) copy-start(bf16[2048,2]{0,1:T(2,128)(2,1)} %param.34) | copy-start | bytes 24580
  6.5 301.9 %copy-start.5 = (s32[8]{0:T(128)S(1)}, s32[8]{0:T(128)}, u32[]{:S(2)}) copy-start(s32[8]{0:T(128)} %param.41) | copy-start | bytes 100
  6.5 158.4 %all-gather.3.cloned.1.call-start = ((), (), s32[]{:S(2)}) async-start(), calls=%async_computation.1 | async-start | bytes 4259840 | tf_op jit(solution)/shard_map/all_gather | solution.py:124
  7.3 301.1 %all-gather.5.cloned.1.call-start = ((), (), s32[]{:S(2)}) async-start(), calls=%async_computation.2 | async-start | bytes 4259840 | tf_op jit(solution)/shard_map/all_gather | solution.py:125
  8.9 346.7 %reduce-scatter.2.cloned.1.call-start = ((), (), s32[]{:S(2)}) async-start(), calls=%async_computation.3 | async-start | bytes 589824 | tf_op jit(solution)/shard_map/reduce_scatter | solution.py:147
  24.4 33.5 %collective-permute-start.9 = (bf16[128,1,128]{2,0,1:T(8,128)(2,1)S(1)}, bf16[128,1,128]{2,0,1:T(8,128)(2,1)S(1)}, u32[]{:S(2)}, u32[]{:S(2)}) collective-permute-start(bf16[128,1,128]{2,0,1:T(8,128)(2,1)S(1)} %bitcast.382), channel_id=1, source_target_pairs={{0,320},{8,328},{16,336},{24,344},{32,352},{40,360},{48,368},{56,3... | collective-permute-start | bytes 98312 | tf_op jit(solution)/shard_map/ppermute | solution.py:16
  41.7 17.5 %collective-permute-start.7 = (bf16[128,1,128]{2,0,1:T(8,128)(2,1)S(1)}, bf16[128,1,128]{2,0,1:T(8,128)(2,1)S(1)}, u32[]{:S(2)}, u32[]{:S(2)}) collective-permute-start(bf16[128,1,128]{2,0,1:T(8,128)(2,1)S(1)} %bitcast.383), channel_id=1, source_target_pairs={{0,256},{8,264},{16,272},{24,280},{32,288},{40,296},{48,304},{56,3... | collective-permute-start | bytes 98312 | tf_op jit(solution)/shard_map/ppermute | solution.py:16
  43.0 18.0 %collective-permute-start.5 = (bf16[128,1,128]{2,0,1:T(8,128)(2,1)S(1)}, bf16[128,1,128]{2,0,1:T(8,128)(2,1)S(1)}, u32[]{:S(2)}, u32[]{:S(2)}) collective-permute-start(bf16[128,1,128]{2,0,1:T(8,128)(2,1)S(1)} %bitcast.384), channel_id=1, source_target_pairs={{0,192},{8,200},{16,208},{24,216},{32,224},{40,232},{48,240},{56,2... | collective-permute-start | bytes 98312 | tf_op jit(solution)/shard_map/ppermute | solution.py:16
  44.3 18.6 %collective-permute-start.3 = (bf16[128,1,128]{2,0,1:T(8,128)(2,1)S(1)}, bf16[128,1,128]{2,0,1:T(8,128)(2,1)S(1)}, u32[]{:S(2)}, u32[]{:S(2)}) collective-permute-start(bf16[128,1,128]{2,0,1:T(8,128)(2,1)S(1)} %bitcast.385), channel_id=1, source_target_pairs={{0,128},{8,136},{16,144},{24,152},{32,160},{40,168},{48,176},{56,1... | collective-permute-start | bytes 98312 | tf_op jit(solution)/shard_map/ppermute | solution.py:16
  46.8 27.8 %collective-permute-start.1 = (bf16[128,1,128]{2,0,1:T(8,128)(2,1)S(1)}, bf16[128,1,128]{2,0,1:T(8,128)(2,1)S(1)}, u32[]{:S(2)}, u32[]{:S(2)}) collective-permute-start(bf16[128,1,128]{2,0,1:T(8,128)(2,1)S(1)} %bitcast.386), channel_id=1, source_target_pairs={{0,64},{8,72},{16,80},{24,88},{32,96},{40,104},{48,112},{56,120},{... | collective-permute-start | bytes 98312 | tf_op jit(solution)/shard_map/ppermute | solution.py:16
  57.9 17.4 %collective-permute-start.6 = (bf16[128,1,128]{0,2,1:T(8,128)(2,1)S(1)}, bf16[128,1,128]{0,2,1:T(8,128)(2,1)S(1)}, u32[]{:S(2)}, u32[]{:S(2)}) collective-permute-start(bf16[128,1,128]{0,2,1:T(8,128)(2,1)S(1)} %pad_maximum_fusion.1), channel_id=1, source_target_pairs={{0,256},{8,264},{16,272},{24,280},{32,288},{40,296},{48,304},{56,3... | collective-permute-start | bytes 98312 | tf_op jit(solution)/shard_map/ppermute | solution.py:16
  59.2 16.7 %collective-permute-start.4 = (bf16[128,1,128]{0,2,1:T(8,128)(2,1)S(1)}, bf16[128,1,128]{0,2,1:T(8,128)(2,1)S(1)}, u32[]{:S(2)}, u32[]{:S(2)}) collective-permute-start(bf16[128,1,128]{0,2,1:T(8,128)(2,1)S(1)} %pad_maximum_fusion.1), channel_id=1, source_target_pairs={{0,192},{8,200},{16,208},{24,216},{32,224},{40,232},{48,240},{56,2... | collective-permute-start | bytes 98312 | tf_op jit(solution)/shard_map/ppermute | solution.py:16
  61.0 15.6 %collective-permute-start.2 = (bf16[128,1,128]{0,2,1:T(8,128)(2,1)S(1)}, bf16[128,1,128]{0,2,1:T(8,128)(2,1)S(1)}, u32[]{:S(2)}, u32[]{:S(2)}) collective-permute-start(bf16[128,1,128]{0,2,1:T(8,128)(2,1)S(1)} %pad_maximum_fusion.1), channel_id=1, source_target_pairs={{0,128},{8,136},{16,144},{24,152},{32,160},{40,168},{48,176},{56,1... | collective-permute-start | bytes 98312 | tf_op jit(solution)/shard_map/ppermute | solution.py:16
  63.0 15.9 %collective-permute-start = (bf16[128,1,128]{0,2,1:T(8,128)(2,1)S(1)}, bf16[128,1,128]{0,2,1:T(8,128)(2,1)S(1)}, u32[]{:S(2)}, u32[]{:S(2)}) collective-permute-start(bf16[128,1,128]{0,2,1:T(8,128)(2,1)S(1)} %pad_maximum_fusion.1), channel_id=1, source_target_pairs={{0,64},{8,72},{16,80},{24,88},{32,96},{40,104},{48,112},{56,120},{... | collective-permute-start | bytes 98312 | tf_op jit(solution)/shard_map/ppermute | solution.py:16
  74.6 7.7 %collective-permute-start.13 = (bf16[128,1,128]{2,0,1:T(8,128)(2,1)S(1)}, bf16[128,1,128]{2,0,1:T(8,128)(2,1)S(1)}, u32[]{:S(2)}, u32[]{:S(2)}) collective-permute-start(bf16[128,1,128]{2,0,1:T(8,128)(2,1)S(1)} %bitcast.387), channel_id=1, source_target_pairs={{0,448},{8,456},{16,464},{24,472},{32,480},{40,488},{48,496},{56,5... | collective-permute-start | bytes 98312 | tf_op jit(solution)/shard_map/ppermute | solution.py:16
  75.3 7.0 %collective-permute-start.11 = (bf16[128,1,128]{2,0,1:T(8,128)(2,1)S(1)}, bf16[128,1,128]{2,0,1:T(8,128)(2,1)S(1)}, u32[]{:S(2)}, u32[]{:S(2)}) collective-permute-start(bf16[128,1,128]{2,0,1:T(8,128)(2,1)S(1)} %bitcast.388), channel_id=1, source_target_pairs={{0,384},{8,392},{16,400},{24,408},{32,416},{40,424},{48,432},{56,4... | collective-permute-start | bytes 98312 | tf_op jit(solution)/shard_map/ppermute | solution.py:16
  76.0 6.3 %collective-permute-start.12 = (bf16[128,1,128]{0,2,1:T(8,128)(2,1)S(1)}, bf16[128,1,128]{0,2,1:T(8,128)(2,1)S(1)}, u32[]{:S(2)}, u32[]{:S(2)}) collective-permute-start(bf16[128,1,128]{0,2,1:T(8,128)(2,1)S(1)} %pad_maximum_fusion.1), channel_id=1, source_target_pairs={{0,448},{8,456},{16,464},{24,472},{32,480},{40,488},{48,496},{56,5... | collective-permute-start | bytes 98312 | tf_op jit(solution)/shard_map/ppermute | solution.py:16
  76.7 5.6 %collective-permute-start.10 = (bf16[128,1,128]{0,2,1:T(8,128)(2,1)S(1)}, bf16[128,1,128]{0,2,1:T(8,128)(2,1)S(1)}, u32[]{:S(2)}, u32[]{:S(2)}) collective-permute-start(bf16[128,1,128]{0,2,1:T(8,128)(2,1)S(1)} %pad_maximum_fusion.1), channel_id=1, source_target_pairs={{0,384},{8,392},{16,400},{24,408},{32,416},{40,424},{48,432},{56,4... | collective-permute-start | bytes 98312 | tf_op jit(solution)/shard_map/ppermute | solution.py:16
  78.9 3.3 collective-permute-start.8
  308.4 47.2 %copy-start.2 = (bf16[128,256]{1,0:T(8,128)(2,1)S(1)}, bf16[128,256]{1,0:T(8,128)(2,1)}, u32[]{:S(2)}) copy-start(bf16[128,256]{1,0:T(8,128)(2,1)} %param.29) | copy-start | bytes 196612
  311.8 5.8 %copy-start.1 = (bf16[2,8192,128]{1,2,0:T(8,128)(2,1)S(1)}, bf16[2,8192,128]{1,2,0:T(8,128)(2,1)}, u32[]{:S(2)}) copy-start(bf16[2,8192,128]{1,2,0:T(8,128)(2,1)} %get-tuple-element.288) | copy-start | bytes 12582916 | tf_op jit(solution)/shard_map/cond
Sparse Core Ops, SparseCore 0:
  10.3 154.5 all-gather.2
  167.8 140.5 all-gather.4
  321.7 33.9 reduce-scatter.1
where the time goes:
time: 364 us
  waiting for transfers between devices  262 us (72%)
  starting transfers between devices  45.5 us (12%)
  between operations  14.9 us (4%)
  matrix products  14.7 us (4%)
  blocking collectives  13.8 us (4%)
  other arithmetic  6.18 us (2%)
  local copies, waits for them, and re-layouts  3.84 us (1%)
    all_gather x1, waiting for transfers between devices, per_device(): values_piece = lax.all_gather(cache_values, 'seq', axis=1, tiled=True)  143 us
    all_gather x1, waiting for transfers between devices, per_device(): keys_piece = lax.all_gather(cache_keys, 'seq', axis=1, tiled=True)  82.6 us
    ppermute x14, starting transfers between devices, shifted(): return lax.ppermute(value, axis, pairs)  45.4 us
    reduce_scatter x1, waiting for transfers between devices, per_device(): lax.psum_scatter(partial_out.astype(jnp.bfloat16), 'tp', scatter_dimensio...  34.1 us
    all_gather x1, blocking collectives, per_device(): gathered = lax.all_gather(hidden_in, 'tp', axis=1, tiled=True)  13.8 us
  transfers between devices with their start and end apart: 17, of which 4 were waited for; matrix products, arithmetic and copies ran while one was open for 3% of the time, Pallas kernels for 0%

commit v1 on v0

--- a/solution.py
+++ b/solution.py
@@ -8,6 +8,10 @@
 norm_eps = 1e-06
 rope_base = 1000000.0
 masked_score = -1e30
+connect_squares = lambda view, mesh_name, out_dim: jnp.concatenate(
+    lax.all_to_all(jnp.stack([view for _ in range(lax.axis_size(mesh_name))], 0), mesh_name, 0, 0),
+    out_dim,
+)
 
 
 def shifted(value, axis, by):
@@ -122,7 +126,7 @@
             state_now,
         )
     keys_piece = lax.all_gather(cache_keys, "seq", axis=1, tiled=True)
-    values_piece = lax.all_gather(cache_values, "seq", axis=1, tiled=True)
+    values_piece = connect_squares(cache_values, "seq", out_dim=1)
     row_count = keys_piece.shape[1]
     keys_block = lax.dynamic_index_in_dim(keys_piece, group_id, 0, keepdims=False).reshape(
         row_count, kv_local, head_dim

time: 364 us -> 343 us (0.942)
  waiting for transfers between devices: 262 us -> 209 us
  starting transfers between devices: 45.5 us -> 74.1 us
  local copies, waits for them, and re-layouts: 3.84 us -> 10.5 us
    ppermute x14, waiting for transfers between devices: 1.63 us -> 161 us  [shifted(): return lax.ppermute(value, axis, pairs)]
    all_gather x1 -> x0, waiting for transfers between devices: 143 us -> none  [per_device(): values_piece = lax.all_gather(cache_values, 'seq', axis=1, tiled=True)]
    all_gather x1, waiting for transfers between devices: 82.6 us -> 0.02 us  [per_device(): keys_piece = lax.all_gather(cache_keys, 'seq', axis=1, tiled=True)]
    all_to_all x0 -> x1, starting transfers between devices: none -> 19 us  [lax.all_to_all(jnp.stack([view for _ in range(lax.axis_size(mesh_name))],...]
    reduce_scatter x1, waiting for transfers between devices: 34.1 us -> 46.6 us  [per_device(): lax.psum_scatter(partial_out.astype(jnp.bfloat16), 'tp', scatter_dimensio...]
    ppermute x14, starting transfers between devices: 45.4 us -> 55 us  [shifted(): return lax.ppermute(value, axis, pairs)]
    reshape x0 -> x1, local copies, waits for them, and re-layouts: none -> 4.79 us  [jnp.concatenate(lax.all_to_all(jnp.stack([view for _ in range(lax.axis_si...]
  transfers between devices with their start and end apart: 17 -> 17, of which waited for: 4 -> 3; matrix products, arithmetic and copies ran while one was open for 3% -> 2% of each run, Pallas kernels for 0% -> 0%
where the time goes in v1:
time: 343 us
  waiting for transfers between devices  209 us (61%)
  starting transfers between devices  74.1 us (22%)
  between operations  15.3 us (4%)
  blocking collectives  13.6 us (4%)
  matrix products  13.4 us (4%)
  local copies, waits for them, and re-layouts  10.5 us (3%)
  other arithmetic  4.87 us (1%)
    ppermute x14, waiting for transfers between devices, shifted(): return lax.ppermute(value, axis, pairs)  161 us
    ppermute x14, starting transfers between devices, shifted(): return lax.ppermute(value, axis, pairs)  55 us
    reduce_scatter x1, waiting for transfers between devices, per_device(): lax.psum_scatter(partial_out.astype(jnp.bfloat16), 'tp', scatter_dimensio...  46.6 us
    all_to_all x1, starting transfers between devices, lax.all_to_all(jnp.stack([view for _ in range(lax.axis_size(mesh_name))],...  19 us
    all_gather x1, blocking collectives, per_device(): gathered = lax.all_gather(hidden_in, 'tp', axis=1, tiled=True)  13.6 us
  transfers between devices with their start and end apart: 17, of which 3 were waited for; matrix products, arithmetic and copies ran while one was open for 2% of the time, Pallas kernels for 0%

profile of v1, /device:TPU:2, one launch (start us, length us, event | category | flops | bytes accessed | tf_op | source)
XLA Modules:
  0.0 342.5 jit_solution(13644375340982271257)
XLA Ops:
  6.5 1.0 copy.87
  7.6 3.0 stack.2
  10.6 19.0 %all-to-all-start = ((bf16[64,2,128,128]{2,3,1,0:T(8,128)(2,1)}), bf16[64,2,128,128]{2,3,1,0:T(8,128)(2,1)}, u32[]{:S(2)}, u32[]{:S(2)}) async-start(bf16[64,2,128,128]{2,3,1,0:T(8,128)(2,1)} %stack.2), calls=%async_computation | async-start | bytes 8388608 | tf_op jit(solution)/shard_map/all_to_all | solution.py:12
  29.7 0.7 all-gather.2.cloned.1.call-update
  30.4 13.6 %all_gather.6 = bf16[128,2048]{1,0:T(8,128)(2,1)S(1)} all-gather(bf16[128,256]{1,0:T(8,128)(2,1)S(1)} %copy-done.2), channel_id=1, replica_groups=mesh['seq'=64,'tp'=8] {'tp'}, dimensions={1}, use_global_device_ids=true | all-gather | bytes 589824 | tf_op jit(solution)/shard_map/all_gather | solution.py:83
  44.1 0.2 fusion.112
  44.3 1.4 convolution_convert_fusion.1
  45.7 13.8 %collective-permute-start.9 = (bf16[128,1,128]{2,0,1:T(8,128)(2,1)S(1)}, bf16[128,1,128]{2,0,1:T(8,128)(2,1)S(1)}, u32[]{:S(2)}, u32[]{:S(2)}) collective-permute-start(bf16[128,1,128]{2,0,1:T(8,128)(2,1)S(1)} %bitcast.388), channel_id=1, source_target_pairs={{0,320},{8,328},{16,336},{24,344},{32,352},{40,360},{48,368},{56,3... | collective-permute-start | bytes 98312 | tf_op jit(solution)/shard_map/ppermute | solution.py:20
  59.5 1.3 collective-permute-start.7
  60.8 1.3 collective-permute-start.5
  62.1 2.5 collective-permute-start.3
  64.6 2.5 collective-permute-start.1
  67.2 0.4 fusion.139
  67.6 0.2 multiply_reduce_fusion
  67.9 0.7 dynamic_slice.27
  69.3 1.5 multiply_reduce_fusion.1
  70.9 0.2 fusion.129
  71.1 0.3 multiply_cosine_fusion
  71.7 0.3 fusion.151
  72.0 0.2 fusion.107
  72.2 0.3 fusion.111
  72.5 157.9 %collective-permute-done.9 = bf16[128,1,128]{2,0,1:T(8,128)(2,1)S(1)} collective-permute-done((bf16[128,1,128]{2,0,1:T(8,128)(2,1)S(1)}, bf16[128,1,128]{2,0,1:T(8,128)(2,1)S(1)}, u32[]{:S(2)}, u32[]{:S(2)}) %collective-permute-start.9) | collective-permute-done | bytes 32800 | tf_op jit(solution)/shard_map/ppermute | solution.py:20
  230.4 14.3 %collective-permute-start.6 = (bf16[128,1,128]{0,2,1:T(8,128)(2,1)S(1)}, bf16[128,1,128]{0,2,1:T(8,128)(2,1)S(1)}, u32[]{:S(2)}, u32[]{:S(2)}) collective-permute-start(bf16[128,1,128]{0,2,1:T(8,128)(2,1)S(1)} %pad_maximum_fusion.1), channel_id=1, source_target_pairs={{0,256},{8,264},{16,272},{24,280},{32,288},{40,296},{48,304},{56,3... | collective-permute-start | bytes 98312 | tf_op jit(solution)/shard_map/ppermute | solution.py:20
  244.8 1.3 collective-permute-start.4
  246.1 3.8 %collective-permute-start.2 = (bf16[128,1,128]{0,2,1:T(8,128)(2,1)S(1)}, bf16[128,1,128]{0,2,1:T(8,128)(2,1)S(1)}, u32[]{:S(2)}, u32[]{:S(2)}) collective-permute-start(bf16[128,1,128]{0,2,1:T(8,128)(2,1)S(1)} %pad_maximum_fusion.1), channel_id=1, source_target_pairs={{0,128},{8,136},{16,144},{24,152},{32,160},{40,168},{48,176},{56,1... | collective-permute-start | bytes 98312 | tf_op jit(solution)/shard_map/ppermute | solution.py:20
  249.9 10.2 %collective-permute-start = (bf16[128,1,128]{0,2,1:T(8,128)(2,1)S(1)}, bf16[128,1,128]{0,2,1:T(8,128)(2,1)S(1)}, u32[]{:S(2)}, u32[]{:S(2)}) collective-permute-start(bf16[128,1,128]{0,2,1:T(8,128)(2,1)S(1)} %pad_maximum_fusion.1), channel_id=1, source_target_pairs={{0,64},{8,72},{16,80},{24,88},{32,96},{40,104},{48,112},{56,120},{... | collective-permute-start | bytes 98312 | tf_op jit(solution)/shard_map/ppermute | solution.py:20
  260.2 0.7 collective-permute-start.13
  260.8 0.7 collective-permute-start.11
  261.5 0.7 collective-permute-start.12
  262.2 0.7 collective-permute-start.10
  262.9 3.3 collective-permute-done
  266.2 1.3 collective-permute-start.8
  268.3 0.6 conditional.8
  268.4 0.2 fusion.144
  268.6 0.2 fusion.1
  268.9 0.5 conditional.9
  269.0 0.2 fusion.145
  269.2 0.2 fusion.12
  269.7 16.7 %conditional.15 = (f32[128,1,2]{0,2,1:T(2,128)S(1)}, f32[128,1,2,128]{0,3,2,1:T(8,128)S(1)}) conditional(s32[]{:T(128)} %convert_element_type.107, (f32[128,1,2]{0,2,1:T(2,128)S(1)}, f32[128,1,2,128]{3,0,2,1:T(8,128)S(1)}) %tuple.71, (s32[]{:T(128)}, s32[8192]{0:T(1024)S(1)}, s32[8]{0:T(128)S(1)}, s32[]{:T(128)}, bf16[2,8192,128]{2,1,0:T(8,128)(2,1)}, ...), branch_computations={%region_33.34_spmd, %region_34.37_spmd} | conditional | flops 1088496640 | bytes 55179364 | solution.py:138
  269.7 0.6 dynamic_slice.23
  272.2 4.8 %copy_bitcast_fusion = bf16[2,8192,128]{1,2,0:T(8,128)(2,1)} fusion(bf16[2,64,128,128]{2,3,0,1:T(8,128)(2,1)} %get-tuple-element.508), kind=kLoop, calls=%fused_computation.121 | loop fusion | bytes 8388608 | tf_op jit(solution)/shard_map/reshape | solution.py:11
  277.0 0.7 broadcast_compare_fusion
  277.8 5.8 %fusion.143 = (f32[128,2]{0,1:T(2,128)S(1)}, f32[128,1,2,8192]{0,3,2,1:T(8,128)S(1)}) fusion(bf16[128,1,2,128]{3,0,2,1:T(8,128)(2,1)S(1)} %get-tuple-element.287, bf16[2,8192,128]{2,1,0:T(8,128)(2,1)} %get-tuple-element.284, s32[]{:T(128)S(6)} %select_n.37, pred[8192]{0:T(1024)(128)(4,1)S(1)} %broadcast_compare_fusion), kind=kOutput, calls=%fused_computation.203 | convolution fusion | flops 543162112 | bytes 10560516 | tf_op jit(solution)/shard_map/cond/branch_1_fun/tcgd,kcd->tcgk/dot_general | solution.py:43
  283.7 1.6 fusion.95
  285.3 1.1 fusion.81
  286.5 1.1 convolution_convert_fusion
  287.6 46.6 %reduce-scatter.2.cloned.1.call-done = bf16[128,256]{1,0:T(8,128)(2,1)} async-done(((bf16[128,2048]{1,0:T(8,128)(2,1)}), bf16[128,256]{1,0:T(8,128)(2,1)}) %reduce-scatter.2.cloned.1.call-update) | async-done | bytes 65552 | tf_op jit(solution)/shard_map/reduce_scatter | solution.py:151
  334.2 1.5 add_convert_fusion
  (72 shorter events, 1.3 us)
Async XLA Ops:
  6.5 279.9 %copy-start = (bf16[256,2048]{1,0:T(8,128)(2,1)S(1)}, bf16[256,2048]{1,0:T(8,128)(2,1)}, u32[]{:S(2)}) copy-start(bf16[256,2048]{1,0:T(8,128)(2,1)} %param.35) | copy-start | bytes 3145732
  10.6 19.8 %copy-start.2 = (bf16[128,256]{1,0:T(8,128)(2,1)S(1)}, bf16[128,256]{1,0:T(8,128)(2,1)}, u32[]{:S(2)}) copy-start(bf16[128,256]{1,0:T(8,128)(2,1)} %param.29) | copy-start | bytes 196612
  10.6 33.7 %copy-start.6 = (f32[2048]{0:T(1024)S(1)}, f32[2048]{0:T(1024)}, u32[]{:S(2)}) copy-start(f32[2048]{0:T(1024)} %param.30) | copy-start | bytes 24580
  10.6 56.6 %copy-start.5 = (bf16[2048,256]{1,0:T(8,128)(2,1)S(1)}, bf16[2048,256]{1,0:T(8,128)(2,1)}, u32[]{:S(2)}) copy-start(bf16[2048,256]{1,0:T(8,128)(2,1)} %param.31) | copy-start | bytes 3145732
  10.6 259.1 %all-to-all-start = ((bf16[64,2,128,128]{2,3,1,0:T(8,128)(2,1)}), bf16[64,2,128,128]{2,3,1,0:T(8,128)(2,1)}, u32[]{:S(2)}, u32[]{:S(2)}) async-start(bf16[64,2,128,128]{2,3,1,0:T(8,128)(2,1)} %stack.2), calls=%async_computation | async-start | bytes 8388608 | tf_op jit(solution)/shard_map/all_to_all | solution.py:12
  29.6 38.3 %copy-start.8 = (s32[8]{0:T(128)S(1)}, s32[8]{0:T(128)}, u32[]{:S(2)}) copy-start(s32[8]{0:T(128)} %param.40) | copy-start | bytes 100
  29.6 41.2 %copy-start.3 = (f32[128]{0:T(128)S(1)}, f32[128]{0:T(128)}, u32[]{:S(2)}) copy-start(f32[128]{0:T(128)} %param.37) | copy-start | bytes 1540
  29.6 41.8 %copy-start.4 = (f32[128]{0:T(128)S(1)}, f32[128]{0:T(128)}, u32[]{:S(2)}) copy-start(f32[128]{0:T(128)} %param.36) | copy-start | bytes 1540
  29.6 42.6 %copy-start.7 = (bf16[2048,2]{0,1:T(2,128)(2,1)S(1)}, bf16[2048,2]{0,1:T(2,128)(2,1)}, u32[]{:S(2)}) copy-start(bf16[2048,2]{0,1:T(2,128)(2,1)} %param.34) | copy-start | bytes 24580
  29.6 240.0 %all-gather.2.cloned.1.call-start = ((), (), s32[]{:S(2)}) async-start(), calls=%async_computation.2 | async-start | bytes 4259840 | tf_op jit(solution)/shard_map/all_gather | solution.py:128
  30.4 303.8 %reduce-scatter.2.cloned.1.call-start = ((), (), s32[]{:S(2)}) async-start(), calls=%async_computation.3 | async-start | bytes 589824 | tf_op jit(solution)/shard_map/reduce_scatter | solution.py:151
  45.7 184.8 %collective-permute-start.9 = (bf16[128,1,128]{2,0,1:T(8,128)(2,1)S(1)}, bf16[128,1,128]{2,0,1:T(8,128)(2,1)S(1)}, u32[]{:S(2)}, u32[]{:S(2)}) collective-permute-start(bf16[128,1,128]{2,0,1:T(8,128)(2,1)S(1)} %bitcast.388), channel_id=1, source_target_pairs={{0,320},{8,328},{16,336},{24,344},{32,352},{40,360},{48,368},{56,3... | collective-permute-start | bytes 98312 | tf_op jit(solution)/shard_map/ppermute | solution.py:20
  59.5 185.3 %collective-permute-start.7 = (bf16[128,1,128]{2,0,1:T(8,128)(2,1)S(1)}, bf16[128,1,128]{2,0,1:T(8,128)(2,1)S(1)}, u32[]{:S(2)}, u32[]{:S(2)}) collective-permute-start(bf16[128,1,128]{2,0,1:T(8,128)(2,1)S(1)} %bitcast.389), channel_id=1, source_target_pairs={{0,256},{8,264},{16,272},{24,280},{32,288},{40,296},{48,304},{56,3... | collective-permute-start | bytes 98312 | tf_op jit(solution)/shard_map/ppermute | solution.py:20
  60.8 185.3 %collective-permute-start.5 = (bf16[128,1,128]{2,0,1:T(8,128)(2,1)S(1)}, bf16[128,1,128]{2,0,1:T(8,128)(2,1)S(1)}, u32[]{:S(2)}, u32[]{:S(2)}) collective-permute-start(bf16[128,1,128]{2,0,1:T(8,128)(2,1)S(1)} %bitcast.390), channel_id=1, source_target_pairs={{0,192},{8,200},{16,208},{24,216},{32,224},{40,232},{48,240},{56,2... | collective-permute-start | bytes 98312 | tf_op jit(solution)/shard_map/ppermute | solution.py:20
  62.1 187.8 %collective-permute-start.3 = (bf16[128,1,128]{2,0,1:T(8,128)(2,1)S(1)}, bf16[128,1,128]{2,0,1:T(8,128)(2,1)S(1)}, u32[]{:S(2)}, u32[]{:S(2)}) collective-permute-start(bf16[128,1,128]{2,0,1:T(8,128)(2,1)S(1)} %bitcast.391), channel_id=1, source_target_pairs={{0,128},{8,136},{16,144},{24,152},{32,160},{40,168},{48,176},{56,1... | collective-permute-start | bytes 98312 | tf_op jit(solution)/shard_map/ppermute | solution.py:20
  64.6 195.5 %collective-permute-start.1 = (bf16[128,1,128]{2,0,1:T(8,128)(2,1)S(1)}, bf16[128,1,128]{2,0,1:T(8,128)(2,1)S(1)}, u32[]{:S(2)}, u32[]{:S(2)}) collective-permute-start(bf16[128,1,128]{2,0,1:T(8,128)(2,1)S(1)} %bitcast.392), channel_id=1, source_target_pairs={{0,64},{8,72},{16,80},{24,88},{32,96},{40,104},{48,112},{56,120},{... | collective-permute-start | bytes 98312 | tf_op jit(solution)/shard_map/ppermute | solution.py:20
  71.7 198.0 %copy-start.9 = (s32[8]{0:T(128)S(1)}, s32[8]{0:T(128)}, u32[]{:S(2)}) copy-start(s32[8]{0:T(128)} %param.41) | copy-start | bytes 100
  230.4 30.4 %collective-permute-start.6 = (bf16[128,1,128]{0,2,1:T(8,128)(2,1)S(1)}, bf16[128,1,128]{0,2,1:T(8,128)(2,1)S(1)}, u32[]{:S(2)}, u32[]{:S(2)}) collective-permute-start(bf16[128,1,128]{0,2,1:T(8,128)(2,1)S(1)} %pad_maximum_fusion.1), channel_id=1, source_target_pairs={{0,256},{8,264},{16,272},{24,280},{32,288},{40,296},{48,304},{56,3... | collective-permute-start | bytes 98312 | tf_op jit(solution)/shard_map/ppermute | solution.py:20
  244.8 16.7 %collective-permute-start.4 = (bf16[128,1,128]{0,2,1:T(8,128)(2,1)S(1)}, bf16[128,1,128]{0,2,1:T(8,128)(2,1)S(1)}, u32[]{:S(2)}, u32[]{:S(2)}) collective-permute-start(bf16[128,1,128]{0,2,1:T(8,128)(2,1)S(1)} %pad_maximum_fusion.1), channel_id=1, source_target_pairs={{0,192},{8,200},{16,208},{24,216},{32,224},{40,232},{48,240},{56,2... | collective-permute-start | bytes 98312 | tf_op jit(solution)/shard_map/ppermute | solution.py:20
  246.1 16.1 %collective-permute-start.2 = (bf16[128,1,128]{0,2,1:T(8,128)(2,1)S(1)}, bf16[128,1,128]{0,2,1:T(8,128)(2,1)S(1)}, u32[]{:S(2)}, u32[]{:S(2)}) collective-permute-start(bf16[128,1,128]{0,2,1:T(8,128)(2,1)S(1)} %pad_maximum_fusion.1), channel_id=1, source_target_pairs={{0,128},{8,136},{16,144},{24,152},{32,160},{40,168},{48,176},{56,1... | collective-permute-start | bytes 98312 | tf_op jit(solution)/shard_map/ppermute | solution.py:20
  249.9 16.3 %collective-permute-start = (bf16[128,1,128]{0,2,1:T(8,128)(2,1)S(1)}, bf16[128,1,128]{0,2,1:T(8,128)(2,1)S(1)}, u32[]{:S(2)}, u32[]{:S(2)}) collective-permute-start(bf16[128,1,128]{0,2,1:T(8,128)(2,1)S(1)} %pad_maximum_fusion.1), channel_id=1, source_target_pairs={{0,64},{8,72},{16,80},{24,88},{32,96},{40,104},{48,112},{56,120},{... | collective-permute-start | bytes 98312 | tf_op jit(solution)/shard_map/ppermute | solution.py:20
  260.2 9.4 %collective-permute-start.13 = (bf16[128,1,128]{2,0,1:T(8,128)(2,1)S(1)}, bf16[128,1,128]{2,0,1:T(8,128)(2,1)S(1)}, u32[]{:S(2)}, u32[]{:S(2)}) collective-permute-start(bf16[128,1,128]{2,0,1:T(8,128)(2,1)S(1)} %bitcast.393), channel_id=1, source_target_pairs={{0,448},{8,456},{16,464},{24,472},{32,480},{40,488},{48,496},{56,5... | collective-permute-start | bytes 98312 | tf_op jit(solution)/shard_map/ppermute | solution.py:20
  260.8 8.7 %collective-permute-start.11 = (bf16[128,1,128]{2,0,1:T(8,128)(2,1)S(1)}, bf16[128,1,128]{2,0,1:T(8,128)(2,1)S(1)}, u32[]{:S(2)}, u32[]{:S(2)}) collective-permute-start(bf16[128,1,128]{2,0,1:T(8,128)(2,1)S(1)} %bitcast.394), channel_id=1, source_target_pairs={{0,384},{8,392},{16,400},{24,408},{32,416},{40,424},{48,432},{56,4... | collective-permute-start | bytes 98312 | tf_op jit(solution)/shard_map/ppermute | solution.py:20
  261.5 8.1 %collective-permute-start.12 = (bf16[128,1,128]{0,2,1:T(8,128)(2,1)S(1)}, bf16[128,1,128]{0,2,1:T(8,128)(2,1)S(1)}, u32[]{:S(2)}, u32[]{:S(2)}) collective-permute-start(bf16[128,1,128]{0,2,1:T(8,128)(2,1)S(1)} %pad_maximum_fusion.1), channel_id=1, source_target_pairs={{0,448},{8,456},{16,464},{24,472},{32,480},{40,488},{48,496},{56,5... | collective-permute-start | bytes 98312 | tf_op jit(solution)/shard_map/ppermute | solution.py:20
  262.2 7.4 %collective-permute-start.10 = (bf16[128,1,128]{0,2,1:T(8,128)(2,1)S(1)}, bf16[128,1,128]{0,2,1:T(8,128)(2,1)S(1)}, u32[]{:S(2)}, u32[]{:S(2)}) collective-permute-start(bf16[128,1,128]{0,2,1:T(8,128)(2,1)S(1)} %pad_maximum_fusion.1), channel_id=1, source_target_pairs={{0,384},{8,392},{16,400},{24,408},{32,416},{40,424},{48,432},{56,4... | collective-permute-start | bytes 98312 | tf_op jit(solution)/shard_map/ppermute | solution.py:20
  266.2 3.3 collective-permute-start.8
  277.8 5.8 %copy-start.1 = (bf16[2,8192,128]{1,2,0:T(8,128)(2,1)S(1)}, bf16[2,8192,128]{1,2,0:T(8,128)(2,1)}, u32[]{:S(2)}) copy-start(bf16[2,8192,128]{1,2,0:T(8,128)(2,1)} %copy_bitcast_fusion) | copy-start | bytes 12582916 | tf_op jit(solution)/shard_map/cond
Sparse Core Ops, SparseCore 0:
  33.4 220.2 all-gather.1
  287.7 46.4 reduce-scatter.1
